TPU v7x, 256 devices: a whole 4x4x8 slice. The times are simulated.
256 devices in a mesh: rows: 64 (over y, z, core), rhs: 4 (over x).
Axes of the slice: x: 4, y: 4, z: 8, core: 2. Of those that a mesh axis runs over, the one named last changes fastest.
Arguments:
- kernel_rows: bfloat16 [131072, 512], P(('rows', 'rhs')), may hold values from 0 to 1
- factor_blocks: bfloat16 [512, 8, 256, 256], P('rows'), may hold values from -0.125 to 0.125
- diag_inverse: bfloat16 [512, 256, 256], P('rows'), as said below
- pattern: int32 [512, 8], P('rows'), may hold values from 0 to 511, as said below
- live_counts: int32 [512], P('rows'), may hold values from 0 to 8, as said below
Outputs:
- solution: bfloat16 [131072, 512], P('rows', 'rhs')
Inputs may be any that keep to these rules, and one draw needn't show every extreme that they name: pattern[s, k] names a block row of a lower level than s; slot 0 of every block row above level 0 names a block row of the level just below; rows of level 0 hold 0. Block row t is held by index t // 8 of rows; the used slots of the block rows held by one index of rows name, for any one level, at most 1 distinct block rows held by any one other index. `live_counts`: 0 on level 0, from 1 to 8 on higher levels, 8 reached. `diag_inverse`: each block is the inverse of a well-conditioned diagonal block of the factor.
All inputs are finite; a program needn't handle non-finite values.
Results may differ from a plain program's by a relative error of at most 0.0058.
Values may be sent and summed in bfloat16 or wider, within the bound.
No kernel may reach another device: no remote copies, remote signals or barrier semaphores. Data moves between devices by JAX's collectives and lax.ppermute only.
A program may use at most 128 MiB of HBM per device.

v0:
```python
import jax
import jax.numpy as jnp
from jax import lax
from jax.sharding import PartitionSpec as P

LEV = 4


def shards(kernel_rows, factor_blocks, diag_inverse, pattern, live_counts):
    received = lax.all_to_all(kernel_rows, "rhs", split_axis=1, concat_axis=0, tiled=True)
    per_device = factor_blocks.shape[0]
    slot_count = factor_blocks.shape[1]
    block = factor_blocks.shape[2]
    width = received.shape[1]
    right_side = received.reshape(per_device, block, width)
    holders = lax.axis_size("rows")
    per_level = per_device // LEV
    level_size = holders * per_level
    level_of = pattern % per_device // per_level
    holder_of = pattern // per_device
    offset_of = pattern % per_level
    active = jnp.arange(slot_count)[None, :] < live_counts[:, None]
    position = holder_of * per_level + offset_of
    flat_index = level_of * level_size + position
    gathered_all = []
    solved_all = []
    for level_now in range(LEV):
        lower = level_now * per_level
        upper = lower + per_level
        if level_now == 0:
            summed_now = jnp.zeros((per_level, block, width), jnp.float32)
        else:
            available = jnp.concatenate(gathered_all, axis=0)
            picked = jnp.take(available, flat_index[lower:upper], axis=0, mode="clip")
            picked = jnp.where(active[lower:upper, :, None, None], picked, jnp.zeros_like(picked))
            summed_now = jnp.einsum(
                "bkij,bkjr->bir",
                factor_blocks[lower:upper],
                picked,
                preferred_element_type=jnp.float32,
            )
        residual = (right_side[lower:upper].astype(jnp.float32) - summed_now).astype(jnp.bfloat16)
        solved = jnp.einsum(
            "bij,bjr->bir", diag_inverse[lower:upper], residual, preferred_element_type=jnp.float32
        ).astype(jnp.bfloat16)
        solved_all.append(solved)
        if level_now + 1 < LEV:
            incoming = lax.all_gather(solved, "rows", axis=0, tiled=True)
            gathered_all.append(incoming)
    return jnp.concatenate(solved_all, axis=0).reshape(per_device * block, width)


def solution(mesh):
    placed = (
        P(("rows", "rhs"), None),
        P("rows", None, None, None),
        P("rows", None, None),
        P("rows", None),
        P("rows"),
    )
    return jax.shard_map(
        shards, mesh=mesh, in_specs=placed, out_specs=P("rows", "rhs"), check_vma=False
    )
```

profile of v0, /device:TPU:1, one launch (start us, length us, event | category | flops | bytes accessed | tf_op | source)
XLA Modules:
  0.0 339.4 jit_solution(18205425547887080133)
XLA Ops:
  6.5 1.3 copy.30
  7.8 13.2 %all_to_all.16 = bf16[512,4,128]{0,2,1:T(8,128)(2,1)S(1)} all-to-all(bf16[512,4,128]{0,2,1:T(8,128)(2,1)S(1)} %bitcast.60), channel_id=1, replica_groups=mesh['rows'=64,'rhs'=4] {'rhs'}, dimensions={1} | all-to-all | bytes 1048576 | tf_op jit(solution)/shard_map/all_to_all | solution.py:10
  21.2 1.8 convolution_convert_fusion
  23.1 0.7 fusion.71
  23.9 0.7 iota_compare_fusion
  24.7 0.1 copy.34
  24.9 84.1 %all-gather.4.cloned.1.call-done = bf16[128,256,128]{2,1,0:T(8,128)(2,1)} async-done(((bf16[2,256,128]{2,1,0:T(8,128)(2,1)}), bf16[128,256,128]{2,1,0:T(8,128)(2,1)}) %all-gather.4.cloned.1.call-update) | async-done | bytes 8388624 | tf_op jit(solution)/shard_map/all_gather | solution.py:48
  109.0 4.1 %gather_fusion = bf16[16,256,128]{2,1,0:T(8,128)(2,1)S(1)} fusion(bf16[128,256,128]{2,1,0:T(8,128)(2,1)} %all-gather.4.cloned.1.call-done, s32[1024]{0:T(1024)S(1)} %pad_clamp_fusion.2), kind=kCustom, calls=%fused_computation | custom fusion | bytes 2097216 | tf_op jit(solution)/shard_map/jit(_take)/gather | solution.py:34
  113.1 0.5 copy.33
  113.7 3.3 fusion.39
  117.1 0.1 copy.36
  117.2 0.8 copy.38
  118.1 79.3 %all-gather.6.cloned.1.call-done = bf16[128,256,128]{2,1,0:T(8,128)(2,1)} async-done(((bf16[2,256,128]{2,1,0:T(8,128)(2,1)}), bf16[128,256,128]{2,1,0:T(8,128)(2,1)}) %all-gather.6.cloned.1.call-update) | async-done | bytes 8388624 | tf_op jit(solution)/shard_map/all_gather | solution.py:48
  197.4 13.9 %pad_maximum_fusion.1 = bf16[256,256,128]{2,1,0:T(8,128)(2,1)} fusion(bf16[128,256,128]{2,1,0:T(8,128)(2,1)} %all-gather.6.cloned.1.call-done, bf16[128,256,128]{2,1,0:T(8,128)(2,1)} %all-gather.4.cloned.1.call-done), kind=kLoop, calls=%fused_computation.4 | loop fusion | flops 8388608 | bytes 33554432 | tf_op jit(solution)/shard_map/concatenate | solution.py:33
  211.3 6.5 %gather_fusion.1 = bf16[16,256,128]{2,1,0:T(8,128)(2,1)S(1)} fusion(bf16[256,256,128]{2,1,0:T(8,128)(2,1)} %pad_maximum_fusion.1, s32[1024]{0:T(1024)S(1)} %pad_clamp_fusion.1), kind=kCustom, calls=%fused_computation.1 | custom fusion | bytes 2097216 | tf_op jit(solution)/shard_map/jit(_take)/gather | solution.py:34
  217.8 0.5 copy.37
  218.4 3.3 fusion.42
  221.9 0.8 copy.42
  222.7 79.4 %all-gather.8.cloned.1.call-done = bf16[128,256,128]{2,1,0:T(8,128)(2,1)} async-done(((bf16[2,256,128]{2,1,0:T(8,128)(2,1)}), bf16[128,256,128]{2,1,0:T(8,128)(2,1)}) %all-gather.8.cloned.1.call-update) | async-done | bytes 8388624 | tf_op jit(solution)/shard_map/all_gather | solution.py:48
  302.1 17.7 %pad_maximum_fusion = bf16[384,256,128]{2,1,0:T(8,128)(2,1)} fusion(bf16[128,256,128]{2,1,0:T(8,128)(2,1)} %all-gather.8.cloned.1.call-done, bf16[128,256,128]{2,1,0:T(8,128)(2,1)} %all-gather.6.cloned.1.call-done, bf16[128,256,128]{2,1,0:T(8,128)(2,1)} %all-gather.4.cloned.1.call-done), kind=kLoop, calls=%fused_computation.3 | loop fusion | flops 25165824 | bytes 50331648 | tf_op jit(solution)/shard_map/concatenate | solution.py:33
  319.9 9.0 %gather_fusion.2 = bf16[16,256,128]{2,1,0:T(8,128)(2,1)S(1)} fusion(bf16[384,256,128]{2,1,0:T(8,128)(2,1)} %pad_maximum_fusion, s32[1024]{0:T(1024)S(1)} %pad_clamp_fusion), kind=kCustom, calls=%fused_computation.2 | custom fusion | bytes 2097216 | tf_op jit(solution)/shard_map/jit(_take)/gather | solution.py:34
  328.8 0.5 copy.41
  329.4 2.6 fusion.45
  332.0 0.9 pad_maximum_fusion.2
  (26 shorter events, 0.9 us)
Async XLA Ops:
  6.5 102.5 %all-gather.4.cloned.1.call-start = ((), (), s32[]{:S(2)}) async-start(), calls=%async_computation.1 | async-start | bytes 8519680 | tf_op jit(solution)/shard_map/all_gather | solution.py:48
  23.0 174.4 %all-gather.6.cloned.1.call-start = ((), (), s32[]{:S(2)}) async-start(), calls=%async_computation.2 | async-start | bytes 8519680 | tf_op jit(solution)/shard_map/all_gather | solution.py:48
  117.0 185.2 %all-gather.8.cloned.1.call-start = ((), (), s32[]{:S(2)}) async-start(), calls=%async_computation.3 | async-start | bytes 8519680 | tf_op jit(solution)/shard_map/all_gather | solution.py:48
  118.1 100.3 %copy-start.3 = (bf16[8,256,256]{2,1,0:T(8,128)(2,1)S(1)}, bf16[8,256,256]{2,1,0:T(8,128)(2,1)}, u32[]{:S(2)}) copy-start(bf16[8,256,256]{2,1,0:T(8,128)(2,1)} %param.7) | copy-start | bytes 3145732
  319.8 12.2 %copy-start = (bf16[2,256,128]{2,1,0:T(8,128)(2,1)S(1)}, bf16[2,256,128]{2,1,0:T(8,128)(2,1)}, u32[]{:S(2)}) copy-start(bf16[2,256,128]{2,1,0:T(8,128)(2,1)} %convolution_convert_fusion) | copy-start | bytes 393220
  319.9 12.2 %copy-start.1 = (bf16[2,256,128]{2,1,0:T(8,128)(2,1)S(1)}, bf16[2,256,128]{2,1,0:T(8,128)(2,1)}, u32[]{:S(2)}) copy-start(bf16[2,256,128]{2,1,0:T(8,128)(2,1)} %fusion.39) | copy-start | bytes 393220
  319.9 12.2 %copy-start.2 = (bf16[2,256,128]{2,1,0:T(8,128)(2,1)S(1)}, bf16[2,256,128]{2,1,0:T(8,128)(2,1)}, u32[]{:S(2)}) copy-start(bf16[2,256,128]{2,1,0:T(8,128)(2,1)} %fusion.42) | copy-start | bytes 393220
Sparse Core Ops, SparseCore 0:
  23.1 85.8 all-gather.3
  117.1 80.2 all-gather.5
  221.8 80.2 all-gather.7
where the time goes:
time: 340 us; the launch traced here: 339 us
  waiting for transfers between devices  243 us (71%)
  other arithmetic  34 us (10%)
  local copies, waits for them, and re-layouts  25 us (7%)
  between operations  13.3 us (4%)
  blocking collectives  13.2 us (4%)
  matrix products  11 us (3%)
    all_gather x3, waiting for transfers between devices, shards(): incoming = lax.all_gather(solved, 'rows', axis=0, tiled=True)  243 us
    concatenate x2, other arithmetic, shards(): available = jnp.concatenate(gathered_all, axis=0)  31.6 us
    gather x6, local copies, waits for them, and re-layouts, shards(): picked = jnp.take(available, flat_index[lower:upper], axis=0, mode='clip')  21.2 us
    all_to_all x1, blocking collectives, shards(): lax.all_to_all(kernel_rows, 'rhs', split_axis=1, concat_axis=0, tiled=True)  13.2 us
    dot_general x4, matrix products, shards(): jnp.einsum('bij,bjr->bir', diag_inverse[lower:upper], residual, preferred...  11 us
  transfers between devices with their start and end apart: 3, of which 3 were waited for; matrix products, arithmetic and copies ran while one was open for 1% of the time, Pallas kernels for 0%

commit v1 on v0

--- a/solution.py
+++ b/solution.py
@@ -45,7 +45,8 @@
         ).astype(jnp.bfloat16)
         solved_all.append(solved)
         if level_now + 1 < LEV:
-            incoming = lax.all_gather(solved, "rows", axis=0, tiled=True)
+            copies = jnp.concatenate([solved] * lax.axis_size("rows"), axis=0)
+            incoming = lax.all_to_all(copies, "rows", 0, 0, tiled=True)
             gathered_all.append(incoming)
     return jnp.concatenate(solved_all, axis=0).reshape(per_device * block, width)
 

time: 340 us -> 788 us (2.32)
  waiting for transfers between devices: 243 us -> 556 us
  local copies, waits for them, and re-layouts: 25 us -> 148 us
  starting transfers between devices: 0.09 us -> 26 us
  between operations: 13.3 us -> 0.28 us
    all_to_all x0 -> x3, waiting for transfers between devices: none -> 556 us  [shards(): incoming = lax.all_to_all(copies, 'rows', 0, 0, tiled=True)]
    all_gather x3 -> x0, waiting for transfers between devices: 243 us -> none  [shards(): incoming = lax.all_gather(solved, 'rows', axis=0, tiled=True)]
    unnamed x9 -> x191, local copies, waits for them, and re-layouts: 1.27 us -> 124 us
    all_to_all x0 -> x3, starting transfers between devices: none -> 26 us  [shards(): incoming = lax.all_to_all(copies, 'rows', 0, 0, tiled=True)]
  transfers between devices with their start and end apart: 3 -> 3, of which waited for: 3 -> 3; matrix products, arithmetic and copies ran while one was open for 1% -> 0% of each run, Pallas kernels for 0% -> 0%
where the time goes in v1:
time: 788 us; the launch traced here: 787 us
  waiting for transfers between devices  556 us (71%)
  local copies, waits for them, and re-layouts  148 us (19%)
  other arithmetic  32.6 us (4%)
  starting transfers between devices  26 us (3%)
  blocking collectives  13.2 us (2%)
  matrix products  11 us (1%)
    all_to_all x3, waiting for transfers between devices, shards(): incoming = lax.all_to_all(copies, 'rows', 0, 0, tiled=True)  556 us
    unnamed x191, local copies, waits for them, and re-layouts  124 us
    concatenate x2, other arithmetic, shards(): available = jnp.concatenate(gathered_all, axis=0)  31.6 us
    all_to_all x3, starting transfers between devices, shards(): incoming = lax.all_to_all(copies, 'rows', 0, 0, tiled=True)  26 us
    gather x6, local copies, waits for them, and re-layouts, shards(): picked = jnp.take(available, flat_index[lower:upper], axis=0, mode='clip')  21.1 us
  transfers between devices with their start and end apart: 3, of which 3 were waited for; matrix products, arithmetic and copies ran while one was open for 0% of the time, Pallas kernels for 0%

profile of v1, /device:TPU:1, one launch (start us, length us, event | category | flops | bytes accessed | tf_op | source)
XLA Modules:
  0.0 786.9 jit_solution(2433841736740285781)
XLA Ops:
  0.0 1.3 copy.16
  1.3 13.2 %all_to_all.31 = bf16[512,4,128]{0,2,1:T(8,128)(2,1)S(1)} all-to-all(bf16[512,4,128]{0,2,1:T(8,128)(2,1)S(1)} %bitcast.64), channel_id=1, replica_groups=mesh['rows'=64,'rhs'=4] {'rhs'}, dimensions={1} | all-to-all | bytes 1048576 | tf_op jit(solution)/shard_map/all_to_all | solution.py:10
  14.6 1.8 constant_dynamic-update-slice_fusion.63
  40.7 0.7 constant_dynamic-update-slice_fusion.25
  56.6 0.7 constant_dynamic-update-slice_fusion.1
  57.9 13.9 %all-to-all-start.1 = ((bf16[128,256,128]{2,1,0:T(8,128)(2,1)}), bf16[128,256,128]{2,1,0:T(8,128)(2,1)}, u32[]{:S(2)}, u32[]{:S(2)}) async-start(bf16[128,256,128]{2,1,0:T(8,128)(2,1)} %constant_dynamic-update-slice_fusion), calls=%async_computation.1 | async-start | bytes 16777216 | tf_op jit(solution)/shard_map/all_to_all | solution.py:49
  72.3 185.3 %all-to-all-done.1 = bf16[128,256,128]{2,1,0:T(8,128)(2,1)} async-done(((bf16[128,256,128]{2,1,0:T(8,128)(2,1)}), bf16[128,256,128]{2,1,0:T(8,128)(2,1)}, u32[]{:S(2)}, u32[]{:S(2)}) %all-to-all-start.1) | async-done | bytes 8388640 | tf_op jit(solution)/shard_map/all_to_all | solution.py:49
  257.6 4.1 gather_fusion
  262.2 3.3 constant_dynamic-update-slice_fusion.127
  289.8 0.7 constant_dynamic-update-slice_fusion.89
  305.6 0.7 constant_dynamic-update-slice_fusion.65
  306.9 6.1 all-to-all-start.2
  313.4 185.4 %all-to-all-done.2 = bf16[128,256,128]{2,1,0:T(8,128)(2,1)} async-done(((bf16[128,256,128]{2,1,0:T(8,128)(2,1)}), bf16[128,256,128]{2,1,0:T(8,128)(2,1)}, u32[]{:S(2)}, u32[]{:S(2)}) %all-to-all-start.2) | async-done | bytes 8388640 | tf_op jit(solution)/shard_map/all_to_all | solution.py:49
  498.8 13.9 %pad_maximum_fusion.1 = bf16[256,256,128]{2,1,0:T(8,128)(2,1)} fusion(bf16[128,256,128]{2,1,0:T(8,128)(2,1)} %all-to-all-done.2, bf16[128,256,128]{2,1,0:T(8,128)(2,1)} %all-to-all-done.1), kind=kLoop, calls=%fused_computation.4 | loop fusion | flops 8388608 | bytes 33554432 | tf_op jit(solution)/shard_map/concatenate | solution.py:33
  512.7 6.5 gather_fusion.1
  519.8 3.3 constant_dynamic-update-slice_fusion.191
  547.3 0.7 constant_dynamic-update-slice_fusion.153
  563.1 0.7 constant_dynamic-update-slice_fusion.129
  564.5 6.1 all-to-all-start.3
  570.9 185.4 %all-to-all-done.3 = bf16[128,256,128]{2,1,0:T(8,128)(2,1)} async-done(((bf16[128,256,128]{2,1,0:T(8,128)(2,1)}), bf16[128,256,128]{2,1,0:T(8,128)(2,1)}, u32[]{:S(2)}, u32[]{:S(2)}) %all-to-all-start.3) | async-done | bytes 8388640 | tf_op jit(solution)/shard_map/all_to_all | solution.py:49
  756.3 17.7 %pad_maximum_fusion = bf16[384,256,128]{2,1,0:T(8,128)(2,1)} fusion(bf16[128,256,128]{2,1,0:T(8,128)(2,1)} %all-to-all-done.3, bf16[128,256,128]{2,1,0:T(8,128)(2,1)} %all-to-all-done.2, bf16[128,256,128]{2,1,0:T(8,128)(2,1)} %all-to-all-done.1), kind=kLoop, calls=%fused_computation.3 | loop fusion | flops 25165824 | bytes 50331648 | tf_op jit(solution)/shard_map/concatenate | solution.py:33
  774.0 8.9 %gather_fusion.2 = bf16[16,256,128]{2,1,0:T(8,128)(2,1)S(1)} fusion(bf16[384,256,128]{2,1,0:T(8,128)(2,1)} %pad_maximum_fusion, s32[1024]{0:T(1024)S(1)} %pad_clamp_fusion), kind=kCustom, calls=%fused_computation.2 | custom fusion | bytes 2097216 | tf_op jit(solution)/shard_map/jit(_take)/gather | solution.py:34
  783.5 2.6 fusion.45
  786.1 0.9 pad_maximum_fusion.2
  (208 shorter events, 123.1 us)
Async XLA Ops:
  57.9 13.9 %copy-start = (s32[8,8]{1,0:T(8,128)S(1)}, s32[8,8]{1,0:T(8,128)}, u32[]{:S(2)}) copy-start(s32[8,8]{1,0:T(8,128)} %param.8) | copy-start | bytes 772
  57.9 14.0 %copy-start.1 = (s32[8]{0:T(128)S(1)}, s32[8]{0:T(128)}, u32[]{:S(2)}) copy-start(s32[8]{0:T(128)} %param.9) | copy-start | bytes 100
  57.9 199.7 %all-to-all-start.1 = ((bf16[128,256,128]{2,1,0:T(8,128)(2,1)}), bf16[128,256,128]{2,1,0:T(8,128)(2,1)}, u32[]{:S(2)}, u32[]{:S(2)}) async-start(bf16[128,256,128]{2,1,0:T(8,128)(2,1)} %constant_dynamic-update-slice_fusion), calls=%async_computation.1 | async-start | bytes 16777216 | tf_op jit(solution)/shard_map/all_to_all | solution.py:49
  306.9 191.9 %all-to-all-start.2 = ((bf16[128,256,128]{2,1,0:T(8,128)(2,1)}), bf16[128,256,128]{2,1,0:T(8,128)(2,1)}, u32[]{:S(2)}, u32[]{:S(2)}) async-start(bf16[128,256,128]{2,1,0:T(8,128)(2,1)} %constant_dynamic-update-slice_fusion.64), calls=%async_computation.2 | async-start | bytes 16777216 | tf_op jit(solution)/shard_map/all_to_all | solution.py:49
  564.5 191.9 %all-to-all-start.3 = ((bf16[128,256,128]{2,1,0:T(8,128)(2,1)}), bf16[128,256,128]{2,1,0:T(8,128)(2,1)}, u32[]{:S(2)}, u32[]{:S(2)}) async-start(bf16[128,256,128]{2,1,0:T(8,128)(2,1)} %constant_dynamic-update-slice_fusion.128), calls=%async_computation.3 | async-start | bytes 16777216 | tf_op jit(solution)/shard_map/all_to_all | solution.py:49
